TPU v7x, 32 devices: a whole 2x2x4 slice. The times are simulated.
32 devices in a mesh: lines: 2 (over x), col: 16 (over z, y, core).
Axes of the slice: x: 2, y: 2, z: 4, core: 2. Of those that a mesh axis runs over, the one named last changes fastest.
Arguments:
- primary: float32 [16, 4, 128, 256], P(None, 'lines', 'col'), parts along dimension 1, may hold values from -6 to 6
- conductivity: float32 [128, 512], P('col', 'lines'), parts along dimension 1, may hold values from 0.1 to 10
- wavenumbers: float32 [16], replicated, may hold values from 0.05 to 1.5
- quadrature: float32 [16], replicated, may hold values from 0.02 to 0.2
- electrodes: int32 [64], P(('lines', 'col')), parts along dimension 0, may hold values from 0 to 127, as said below
- far_pole: int32 [4, 32], P('lines'), parts along dimension 0, may hold values from 0 to 31, as said below
- observed: float32 [4, 32], P('lines'), parts along dimension 0, may hold values from -6 to 6
- prior_adjoint: float32 [16, 4, 128, 256], P(None, 'lines', 'col'), parts along dimension 1, may hold values from -0.012 to 0.012
Outputs:
- predicted: float32 [4, 32], P('lines'), parts along dimension 0
- gradient: float32 [128, 512], P('col', 'lines'), parts along dimension 1
There are 2 independent parts, one for each index of `lines`. A program takes and returns all parts, laid end to end along the dimension named above; an argument that names none is the same for every part. Nothing has to cross between parts.
Inputs may be any that keep to these rules, and one draw needn't show every extreme that they name: electrodes[e] lies in columns 4 e to 4 e + 3. far_pole[s, r] differs from r by 1 to 8.
All inputs are finite; a program needn't handle non-finite values.
Results may differ from a plain program's by a relative error of at most 0.0003.
Values sent between devices are 32-bit elements; how exact they have to be, the bound alone decides.
No kernel may reach another device: no remote copies, remote signals or barrier semaphores. Data moves between devices by JAX's collectives and lax.ppermute only.
A program may use at most 64 MiB of HBM per device.

v0:
```python
import math
import jax
import jax.numpy as jnp
from jax import lax
from jax.sharding import Mesh
from jax.sharding import PartitionSpec as P

ITERS = 2


def halo(block, axis, dim, width):
    count = lax.axis_size(axis)
    edge_shape = list(block.shape)
    edge_shape[dim] = width
    if count == 1:
        zeros = jnp.zeros(edge_shape, block.dtype)
        return jnp.concatenate([zeros, block, zeros], axis=dim)
    forward = [(i, i + 1) for i in range(count - 1)]
    backward = [(target, source) for source, target in forward]
    low = lax.ppermute(
        lax.slice_in_dim(block, block.shape[dim] - width, None, axis=dim), axis, forward
    )
    high = lax.ppermute(lax.slice_in_dim(block, 0, width, axis=dim), axis, backward)
    return jnp.concatenate([low, block, high], axis=dim)


def next_column(field, axis):
    count = lax.axis_size(axis)
    if count == 1:
        edge = jnp.zeros_like(field[:, :, :1])
    else:
        edge = lax.ppermute(field[:, :, :1], axis, [(i + 1, i) for i in range(count - 1)])
    return jnp.concatenate([field[:, :, 1:], edge], axis=2)


def coefficients(sigma_wide):
    center = sigma_wide[1:-1]
    west_face = 0.5 * (center + sigma_wide[:-2])
    east_face = 0.5 * (center + sigma_wide[2:])
    below_sigma = jnp.concatenate([center[:, 1:], jnp.zeros_like(center[:, :1])], axis=1)
    lower_face = 0.5 * (center + below_sigma)
    above_sigma = jnp.concatenate([jnp.zeros_like(center[:, :1]), center[:, :-1]], axis=1)
    upper_face = 0.5 * (center + above_sigma)
    top_row = jnp.arange(center.shape[1]) == 0
    upper_face = jnp.where(top_row[None, :], 0.0, upper_face)
    return (west_face, east_face, lower_face, upper_face, center)


def stencil(field_wide, faces_set, mass_scale):
    west_face, east_face, lower_face, upper_face, center = faces_set
    middle = field_wide[..., 1:-1, :]
    below_cells = jnp.concatenate([middle[..., 1:], jnp.zeros_like(middle[..., :1])], axis=-1)
    above_cells = jnp.concatenate([jnp.zeros_like(middle[..., :1]), middle[..., :-1]], axis=-1)
    result = west_face * (middle - field_wide[..., :-2, :]) + east_face * (
        middle - field_wide[..., 2:, :]
    )
    result = result + lower_face * (middle - below_cells) + upper_face * (middle - above_cells)
    return result + mass_scale * center * middle


def on_device(
    primary, conductivity, wavenumbers, quadrature, electrodes, far_pole, observed, prior_adjoint
):
    groups = lax.axis_size("kq")
    spread = lax.axis_size("cs")
    waves, sources, own_columns, depth = primary.shape
    per_group = waves // groups
    group = lax.axis_index("kq")
    block = lax.axis_index("cs")
    fields = per_group * sources

    def by_group(array):
        return array.reshape(groups, fields, own_columns, depth)

    sigma_copies = jnp.broadcast_to(conductivity[None, None], (groups, 1, own_columns, depth))
    send = jnp.concatenate([by_group(primary), by_group(prior_adjoint), sigma_copies], axis=1)
    if groups > 1:
        send = lax.all_to_all(send, "kq", 0, 2, tiled=True)
    received = send[0]
    width = groups * own_columns
    primary = received[:fields].reshape(per_group, sources, width, depth)
    prior_adjoint = received[fields : 2 * fields].reshape(per_group, sources, width, depth)
    sigma = received[2 * fields]
    columns = width * spread
    offset = block * width
    wide_sigma = halo(sigma, "cs", 0, 2)
    positions = offset - 2 + jnp.arange(width + 4)
    inside = (positions >= 0) & (positions < columns)
    contrast_wide = jnp.where(inside[:, None], wide_sigma - 1.0, 0.0)
    own_waves = lax.dynamic_slice_in_dim(wavenumbers, group * per_group, per_group)
    weights = lax.dynamic_slice_in_dim(quadrature, group * per_group, per_group)
    mass_scale = (own_waves * own_waves)[:, None, None, None]
    operator_faces = coefficients(wide_sigma[1:-1])

    def operate(state):
        return stencil(halo(state, "cs", 2, 1), operator_faces, mass_scale)

    def dots(left, right):
        total = jnp.sum(left * right, axis=(2, 3))
        if spread > 1:
            total = lax.psum(total, "cs")
        return total[:, :, None, None]

    def conjugate(source, start):
        if start is None:
            solution = jnp.zeros_like(source)
            residual = source
        else:
            solution = start
            residual = source - operate(start)
        direction = residual
        norm_now = dots(residual, residual)
        for iteration in range(ITERS):
            applied = operate(direction)
            step_size = norm_now / dots(direction, applied)
            solution = solution + step_size * direction
            if iteration + 1 < ITERS:
                residual = residual - step_size * applied
                norm_next = dots(residual, residual)
                direction = residual + norm_next / norm_now * direction
                norm_now = norm_next
        return solution

    source = -stencil(halo(primary, "cs", 2, 1), coefficients(contrast_wide[1:-1]), mass_scale)
    total_field = primary + conjugate(source, None)
    surface = total_field[:, :, :, 0]
    weighted = jnp.sum(weights[:, None, None] * surface, axis=0)
    packet = jnp.concatenate([weighted.reshape(-1), electrodes.astype(jnp.float32)])
    gathered = lax.all_gather(packet, ("cs", "kq"))
    partial = gathered[:, : sources * width].reshape(spread, groups, sources, width)
    line_surface = jnp.sum(partial, axis=1).transpose(1, 0, 2).reshape(sources, columns)
    all_electrodes = gathered[:, sources * width :].reshape(-1).astype(jnp.int32)
    count = all_electrodes.shape[0]
    picks = (all_electrodes[:, None] == jnp.arange(columns)[None, :]).astype(jnp.float32)
    potentials = jnp.sum(line_surface[:, None, :] * picks[None], axis=2)
    pole_hits = (far_pole[:, :, None] == jnp.arange(count)[None, None, :]).astype(jnp.float32)
    far_potentials = jnp.sum(potentials[:, None, :] * pole_hits, axis=2)
    predicted = potentials - far_potentials
    misfit = predicted - observed
    returned = jnp.sum(misfit[:, :, None] * pole_hits, axis=1)
    charge = misfit - returned
    own_picks = (all_electrodes[:, None] == offset + jnp.arange(width)[None, :]).astype(jnp.float32)
    charge_cols = jnp.sum(charge[:, :, None] * own_picks[None], axis=1)
    surface_row = (jnp.arange(depth) == 0).astype(jnp.float32)
    adjoint_source = weights[:, None, None, None] * charge_cols[None, :, :, None] * surface_row
    adjoint = conjugate(adjoint_source, prior_adjoint)
    adjoint_next = next_column(adjoint, "cs")
    total_next = next_column(total_field, "cs")
    adjoint_down = jnp.concatenate([adjoint[..., 1:], jnp.zeros_like(adjoint[..., :1])], axis=-1)
    total_down = jnp.concatenate(
        [total_field[..., 1:], jnp.zeros_like(total_field[..., :1])], axis=-1
    )
    correlation = (adjoint_next - adjoint) * (total_next - total_field)
    correlation = correlation + (adjoint_down - adjoint) * (total_down - total_field)
    correlation = correlation + mass_scale * adjoint * total_field
    gradient = jnp.sum(correlation, axis=(0, 1))
    if groups > 1:
        gradient = lax.psum_scatter(gradient, "kq", scatter_dimension=0, tiled=True)
    return (predicted, gradient)


def solution(mesh):
    lines = mesh.shape["lines"]
    col = mesh.shape["col"]

    def run(*arrays):
        groups = math.gcd(col, arrays[0].shape[0])
        split = Mesh(mesh.devices.reshape(lines, col // groups, groups), ("lines", "cs", "kq"))
        cells = ("cs", "kq")
        placed = (
            P(None, "lines", cells, None),
            P(cells, "lines"),
            P(),
            P(),
            P(("lines",) + cells),
            P("lines", None),
            P("lines", None),
            P(None, "lines", cells, None),
        )
        return jax.shard_map(
            on_device,
            mesh=split,
            in_specs=placed,
            out_specs=(P("lines", None), P(cells, "lines")),
            check_vma=False,
        )(*arrays)

    return run
```

profile of v0, /device:TPU:0, one launch (start us, length us, event | category | flops | bytes accessed | tf_op | source)
XLA Modules:
  0.0 163.5 jit_solution(5212997132904193159)
XLA Ops:
  7.2 0.7 broadcast_in_dim.34
  7.9 1.9 %pad_maximum_fusion = f32[16,5,8,256]{3,2,1,0:T(8,128)} fusion(f32[16,1,8,256]{3,2,1,0:T(8,128)S(1)} %broadcast_in_dim.34, f32[16,2,8,256]{3,2,1,0:T(8,128)} %param.15, f32[16,2,8,256]{3,2,1,0:T(8,128)} %param.8), kind=kLoop, calls=%fused_computation | loop fusion | flops 327680 | bytes 1310720 | tf_op jit(solution)/shard_map/concatenate | solution.py:76
  9.8 7.4 %all-to-all-start = ((f32[16,5,8,256]{3,2,1,0:T(8,128)}), f32[16,5,8,256]{3,2,1,0:T(8,128)S(1)}, u32[]{:S(2)}, u32[]{:S(2)}) async-start(f32[16,5,8,256]{3,2,1,0:T(8,128)} %pad_maximum_fusion), calls=%async_computation | async-start | bytes 1310720 | tf_op jit(solution)/shard_map/all_to_all | solution.py:78
  17.3 0.6 copy-done.2
  17.9 0.6 dynamic_slice.7
  19.8 0.6 dynamic_slice.6
  20.4 0.7 copy-done.4
  21.1 0.7 copy-done.5
  21.8 0.6 dynamic-slice
  23.0 10.8 %all-to-all-done = f32[16,5,8,256]{3,2,1,0:T(8,128)S(1)} async-done(((f32[16,5,8,256]{3,2,1,0:T(8,128)}), f32[16,5,8,256]{3,2,1,0:T(8,128)S(1)}, u32[]{:S(2)}, u32[]{:S(2)}) %all-to-all-start) | async-done | bytes 655392 | tf_op jit(solution)/shard_map/all_to_all | solution.py:78
  33.9 0.1 fusion.75
  34.1 0.1 fusion.53
  34.2 0.1 fusion.74
  34.3 0.2 fusion.70
  34.5 0.1 fusion.60
  34.6 0.2 fusion.66
  34.8 0.1 fusion.72
  35.0 0.3 multiply_reduce_fusion.4
  35.3 0.2 multiply_reduce_fusion.3
  35.5 0.1 multiply_add_fusion.2
  35.6 0.1 fusion.71
  35.8 0.3 fusion.52
  36.1 0.1 add_add_fusion
  36.2 0.7 fusion.58
  36.9 0.1 maximum_dynamic-update-slice_fusion
  37.1 60.8 %all-reduce.34 = f32[4128]{0:T(1024)S(1)} all-reduce(f32[4128]{0:T(1024)S(1)} %maximum_dynamic-update-slice_fusion), channel_id=2, replica_groups=mesh['lines'=2,'col'=16] {'col'}, use_global_device_ids=true, to_apply=%add.34 | all-reduce | flops 4128 | bytes 33024
  97.9 0.1 reshape.273
  98.0 0.1 convert_element_type.35
  98.2 0.1 multiply_reduce_fusion.7
  98.3 0.6 copy-done
  98.8 0.2 select_reduce_fusion.1
  99.0 0.5 copy-done.1
  99.5 0.6 fusion.64
  100.1 0.1 select_reduce_fusion
  100.2 0.1 multiply_reduce_fusion.6
  100.3 0.6 broadcast_multiply_fusion.1
  100.9 0.2 fusion.31
  101.1 0.1 fusion.69
  101.3 0.3 multiply_reduce_fusion.1
  101.6 0.2 multiply_reduce_fusion
  101.8 0.1 multiply_add_fusion.1
  101.9 0.1 fusion.68
  102.1 0.3 fusion.51
  102.4 0.1 multiply_add_fusion
  102.5 0.1 slice.227
  102.7 0.1 slice.228
  102.8 0.8 add_reduce_fusion
  103.6 53.0 %reduce-scatter.2.cloned.1.call-done = f32[8,256]{1,0:T(8,128)} async-done(((f32[128,256]{1,0:T(8,128)}), f32[8,256]{1,0:T(8,128)}) %reduce-scatter.2.cloned.1.call-update) | async-done | bytes 8208 | tf_op jit(solution)/shard_map/reduce_scatter | solution.py:158
  (31 shorter events, 0.4 us)
Async XLA Ops:
  9.8 24.0 %all-to-all-start = ((f32[16,5,8,256]{3,2,1,0:T(8,128)}), f32[16,5,8,256]{3,2,1,0:T(8,128)S(1)}, u32[]{:S(2)}, u32[]{:S(2)}) async-start(f32[16,5,8,256]{3,2,1,0:T(8,128)} %pad_maximum_fusion), calls=%async_computation | async-start | bytes 1310720 | tf_op jit(solution)/shard_map/all_to_all | solution.py:78
  17.2 139.4 %reduce-scatter.2.cloned.1.call-start = ((), (), s32[]{:S(2)}) async-start(), calls=%async_computation.2 | async-start | bytes 139264 | tf_op jit(solution)/shard_map/reduce_scatter | solution.py:158
  17.3 0.7 copy-start.2
  18.5 1.3 copy-start.3
  20.4 0.7 copy-start.4
  21.1 0.7 copy-start.5
  98.2 0.7 copy-start
  98.8 0.7 copy-start.1
Sparse Core Ops, SparseCore 0:
  103.7 52.8 reduce-scatter.1
where the time goes:
time: 164 us; the launch traced here: 163 us
  waiting for transfers between devices  63.8 us (39%)
  blocking collectives  60.8 us (37%)
  between operations  16.3 us (10%)
  other arithmetic  8.09 us (5%)
  starting transfers between devices  7.45 us (5%)
  local copies, waits for them, and re-layouts  7.03 us (4%)
    unnamed x1, blocking collectives  60.8 us
    reduce_scatter x1, waiting for transfers between devices, on_device(): gradient = lax.psum_scatter(gradient, 'kq', scatter_dimension=0, tiled=True)  53 us
    all_to_all x1, waiting for transfers between devices, on_device(): send = lax.all_to_all(send, 'kq', 0, 2, tiled=True)  10.8 us
    all_to_all x1, starting transfers between devices, on_device(): send = lax.all_to_all(send, 'kq', 0, 2, tiled=True)  7.41 us
    unnamed x14, local copies, waits for them, and re-layouts  3.66 us
  transfers between devices with their start and end apart: 2, of which 2 were waited for; matrix products, arithmetic and copies ran while one was open for 1% of the time, Pallas kernels for 0%

commit v1 on v0

--- a/solution.py
+++ b/solution.py
@@ -6,6 +6,13 @@
 from jax.sharding import PartitionSpec as P
 
 ITERS = 2
+
+
+def cover_the_floor(block_in):
+    return jnp.concatenate(
+        lax.all_to_all(jnp.stack(jnp.split(block_in, lax.axis_size("kq"), axis=0)), "kq", 0, 0),
+        axis=2,
+    )
 
 
 def halo(block, axis, dim, width):
@@ -75,7 +82,7 @@
     sigma_copies = jnp.broadcast_to(conductivity[None, None], (groups, 1, own_columns, depth))
     send = jnp.concatenate([by_group(primary), by_group(prior_adjoint), sigma_copies], axis=1)
     if groups > 1:
-        send = lax.all_to_all(send, "kq", 0, 2, tiled=True)
+        send = cover_the_floor(send)
     received = send[0]
     width = groups * own_columns
     primary = received[:fields].reshape(per_group, sources, width, depth)

time: 164 us -> 173 us (1.055)
  local copies, waits for them, and re-layouts: 7.03 us -> 16.3 us
    unnamed x14 -> x29, local copies, waits for them, and re-layouts: 3.66 us -> 12.3 us
where the time goes in v1:
time: 173 us; the launch traced here: 172 us
  waiting for transfers between devices  64.4 us (37%)
  blocking collectives  60.8 us (35%)
  local copies, waits for them, and re-layouts  16.3 us (9%)
  between operations  16.3 us (9%)
  starting transfers between devices  7.45 us (4%)
  other arithmetic  7.24 us (4%)
    unnamed x1, blocking collectives  60.8 us
    reduce_scatter x1, waiting for transfers between devices, on_device(): gradient = lax.psum_scatter(gradient, 'kq', scatter_dimension=0, tiled=True)  53 us
    unnamed x29, local copies, waits for them, and re-layouts  12.3 us
    all_to_all x1, waiting for transfers between devices, cover_the_floor(): lax.all_to_all(jnp.stack(jnp.split(block_in, lax.axis_size('kq'), axis=0)...  11.4 us
    all_to_all x1, starting transfers between devices, cover_the_floor(): lax.all_to_all(jnp.stack(jnp.split(block_in, lax.axis_size('kq'), axis=0)...  7.41 us
  transfers between devices with their start and end apart: 2, of which 2 were waited for; matrix products, arithmetic and copies ran while one was open for 1% of the time, Pallas kernels for 0%

profile of v1, /device:TPU:0, one launch (start us, length us, event | category | flops | bytes accessed | tf_op | source)
XLA Modules:
  0.0 172.5 jit_solution(5868692386749008612)
XLA Ops:
  7.2 0.7 broadcast_in_dim.34
  7.9 1.1 pad_maximum_fusion
  9.0 0.6 fusion.76
  9.6 0.6 fusion.75
  10.2 0.6 fusion.74
  10.8 0.6 fusion.73
  11.4 0.6 fusion.72
  12.0 0.6 fusion.71
  12.6 0.6 fusion.70
  13.3 0.6 fusion.69
  13.9 0.6 fusion.68
  14.5 0.6 fusion.67
  15.1 0.6 fusion.66
  15.7 0.6 fusion.65
  16.3 0.6 fusion.64
  17.0 0.6 fusion.63
  17.6 0.6 fusion.62
  18.2 0.6 fusion.61
  18.8 7.4 %all-to-all-start = ((f32[16,1,5,8,256]{4,3,2,1,0:T(8,128)}), f32[16,1,5,8,256]{4,3,2,1,0:T(8,128)S(1)}, u32[]{:S(2)}, u32[]{:S(2)}) async-start(f32[16,1,5,8,256]{4,3,2,1,0:T(8,128)} %fusion.61), calls=%async_computation | async-start | bytes 1310720 | tf_op jit(solution)/shard_map/all_to_all | solution.py:13
  26.3 0.6 copy-done.2
  26.9 0.7 copy-done.3
  27.6 0.6 dynamic_slice.7
  29.5 0.6 dynamic_slice.6
  30.2 0.6 dynamic-slice
  31.4 11.4 %all-to-all-done = f32[16,1,5,8,256]{4,3,2,1,0:T(8,128)S(1)} async-done(((f32[16,1,5,8,256]{4,3,2,1,0:T(8,128)}), f32[16,1,5,8,256]{4,3,2,1,0:T(8,128)S(1)}, u32[]{:S(2)}, u32[]{:S(2)}) %all-to-all-start) | async-done | bytes 655392 | tf_op jit(solution)/shard_map/all_to_all | solution.py:13
  43.3 0.2 fusion.86
  43.5 0.1 fusion.60
  43.6 0.2 fusion.82
  43.8 0.1 fusion.88
  44.0 0.3 multiply_reduce_fusion.4
  44.3 0.2 multiply_reduce_fusion.3
  44.5 0.1 multiply_add_fusion.2
  44.6 0.1 fusion.87
  44.8 0.3 fusion.52
  45.2 0.7 fusion.58
  46.1 60.8 %all-reduce.34 = f32[4128]{0:T(1024)S(1)} all-reduce(f32[4128]{0:T(1024)S(1)} %maximum_dynamic-update-slice_fusion), channel_id=2, replica_groups=mesh['lines'=2,'col'=16] {'col'}, use_global_device_ids=true, to_apply=%add.34 | all-reduce | flops 4128 | bytes 33024
  107.4 0.6 copy-done
  108.0 0.2 select_reduce_fusion.1
  108.2 0.5 copy-done.1
  108.7 0.6 fusion.80
  109.4 0.6 broadcast_multiply_fusion.1
  110.1 0.2 fusion.31
  110.3 0.1 fusion.85
  110.4 0.3 multiply_reduce_fusion.1
  110.7 0.2 multiply_reduce_fusion
  111.2 0.3 fusion.51
  111.8 0.8 add_reduce_fusion
  112.6 53.0 %reduce-scatter.2.cloned.1.call-done = f32[8,256]{1,0:T(8,128)} async-done(((f32[128,256]{1,0:T(8,128)}), f32[8,256]{1,0:T(8,128)}) %reduce-scatter.2.cloned.1.call-update) | async-done | bytes 8208 | tf_op jit(solution)/shard_map/reduce_scatter | solution.py:165
  (47 shorter events, 2.1 us)
Async XLA Ops:
  18.8 24.0 %all-to-all-start = ((f32[16,1,5,8,256]{4,3,2,1,0:T(8,128)}), f32[16,1,5,8,256]{4,3,2,1,0:T(8,128)S(1)}, u32[]{:S(2)}, u32[]{:S(2)}) async-start(f32[16,1,5,8,256]{4,3,2,1,0:T(8,128)} %fusion.61), calls=%async_computation | async-start | bytes 1310720 | tf_op jit(solution)/shard_map/all_to_all | solution.py:13
  26.2 139.4 %reduce-scatter.2.cloned.1.call-start = ((), (), s32[]{:S(2)}) async-start(), calls=%async_computation.2 | async-start | bytes 139264 | tf_op jit(solution)/shard_map/reduce_scatter | solution.py:165
  26.3 0.7 copy-start.2
  26.9 0.7 copy-start.3
  28.2 1.3 copy-start.4
  29.5 0.7 copy-start.5
  107.3 0.7 copy-start
  108.0 0.7 copy-start.1
Sparse Core Ops, SparseCore 0:
  112.7 52.8 reduce-scatter.1
